TPU v7x, 32 devices: a whole 2x2x4 slice. The times are simulated.
32 devices in a mesh: req: 8 (over z, y), tp: 4 (over x, core).
Axes of the slice: x: 2, y: 2, z: 4, core: 2. Of those that a mesh axis runs over, the one named last changes fastest.
Arguments:
- hidden: bfloat16 [4096, 2048], P('req', 'tp'), may hold values from -6 to 6
- queries: bfloat16 [4096, 2048], P('req', 'tp'), may hold values from -4 to 4
- new_keys: bfloat16 [4096, 512], P('req'), may hold values from -4 to 4
- new_values: bfloat16 [4096, 512], P('req'), may hold values from -6 to 6
- cache_keys: bfloat16 [384, 64, 512], P('req'), may hold values from -6 to 6
- cache_values: bfloat16 [384, 64, 512], P('req'), may hold values from -6 to 6
- out_weight: bfloat16 [2048, 2048], P('tp'), may hold values from -0.125 to 0.125
- attn_gain: bfloat16 [2048], P('tp'), may hold values from 0.099609375 to 1.8984375
- ple_input: bfloat16 [4096, 256], P('req'), may hold values from -6 to 6
- ple_gate_weight: bfloat16 [2048, 256], P('tp'), may hold values from -0.125 to 0.125
- ple_proj_weight: bfloat16 [256, 2048], P(None, 'tp'), may hold values from -0.375 to 0.375
- ple_gain: bfloat16 [2048], P('tp'), may hold values from 0.099609375 to 1.8984375
- page_holder: int32 [384, 1], P('req'), may hold values from 0 to 7; in each aligned block of 48 rows (0 to 47, 48 to 95, ...) at most 6 rows name the same one
- page_slot: int32 [384, 1], P('req'), may hold values from 0 to 47
- page_counts: int32 [8, 8], P('req'), may hold values from 1 to 12, 48 in all within a row
- last_fill: int32 [8, 8], P('req'), may hold values from 1 to 64
- row_counts: int32 [8, 8], P('req'), may hold values from 1 to 256, 512 in all within a row
Outputs:
- layer_out: bfloat16 [4096, 2048], P('req', 'tp')
Inputs may be any that keep to these rules, and one draw needn't show every extreme that they name: `page_holder`: within the 48 page references of one device's requests (aligned blocks), no req index is named more than 6 times; in some block one is named exactly 6 times. `page_counts`: the 8 counts of one device sum to 48; some count equals 12. `row_counts`: the 8 counts of one device sum to 512; some count equals 256.
All inputs are finite; a program needn't handle non-finite values.
Results may differ from a plain program's by a relative error of at most 0.0061.
Values may be sent and summed in bfloat16 or wider, within the bound.
No kernel may reach another device: no remote copies, remote signals or barrier semaphores. Data moves between devices by JAX's collectives and lax.ppermute only.
A program may use at most 128 MiB of HBM per device.

v0:
```python
import math
import jax
import jax.numpy as jnp
from jax import lax
from jax.sharding import PartitionSpec as P

D = 2048
HD = 256


def slot_lookup(positions, counts):
    starts = jnp.cumsum(counts) - counts
    owning = jnp.sum((positions[:, None] >= starts[None, :]).astype(jnp.int32), axis=1) - 1
    return (owning, starts)


def table_pick(table, owning):
    onehot = owning[:, None] == jnp.arange(table.shape[0], dtype=jnp.int32)[None, :]
    return jnp.sum(jnp.where(onehot, table[None, :], 0), axis=1)


def attend_masks(counts_of_pages, fill_row, counts_of_rows, page_len, page_total, row_total):
    key_index = jnp.arange(page_total * page_len, dtype=jnp.int32)
    page_ref = key_index // page_len
    within = key_index % page_len
    page_owner, page_starts = slot_lookup(page_ref, counts_of_pages)
    context_len = (counts_of_pages - 1) * page_len + fill_row
    position = (page_ref - table_pick(page_starts, page_owner)) * page_len + within
    valid = position < table_pick(context_len, page_owner)
    row_index = jnp.arange(row_total, dtype=jnp.int32)
    row_owner = slot_lookup(row_index, counts_of_rows)[0]
    context_mask = (row_owner[:, None] == page_owner[None, :]) & valid[None, :]
    causal = (row_owner[:, None] == row_owner[None, :]) & (row_index[None, :] <= row_index[:, None])
    return jnp.concatenate([context_mask, causal], axis=1)


def shards(
    hidden,
    queries,
    new_keys,
    new_values,
    cache_keys,
    cache_values,
    out_weight,
    attn_gain,
    ple_input,
    ple_gate_weight,
    ple_proj_weight,
    ple_gain,
    page_holder,
    page_slot,
    page_counts,
    last_fill,
    row_counts,
):
    row_total = hidden.shape[0]
    page_total = cache_keys.shape[0]
    page_len = cache_keys.shape[1]
    req_count = lax.axis_size("req")
    tp_index = lax.axis_index("tp")
    local_heads = queries.shape[1] // HD
    kv_head = tp_index // 2
    capacity = max(2, page_total // req_count)
    holders = page_holder[:, 0]
    places = page_slot[:, 0]
    ref_index = jnp.arange(page_total, dtype=jnp.int32)
    earlier = (holders[:, None] == holders[None, :]) & (ref_index[:, None] > ref_index[None, :])
    ranking = jnp.sum(earlier.astype(jnp.int32), axis=1)
    matched = (holders[:, None, None] == jnp.arange(req_count, dtype=jnp.int32)[None, :, None]) & (
        ranking[:, None, None] == jnp.arange(capacity, dtype=jnp.int32)[None, None, :]
    )
    request_table = jnp.sum(jnp.where(matched, places[:, None, None] + 1, 0), axis=0) - 1
    asked = lax.all_to_all(request_table, "req", split_axis=0, concat_axis=0, tiled=True)
    wanted = jnp.maximum(asked, 0)
    head_keys = lax.dynamic_slice_in_dim(cache_keys, kv_head * HD, HD, 2)
    head_values = lax.dynamic_slice_in_dim(cache_values, kv_head * HD, HD, 2)
    stacked = jnp.concatenate([head_keys, head_values], axis=2)
    arrival_index = holders * capacity + ranking
    outgoing = stacked[wanted]
    arrived = lax.all_to_all(outgoing, "req", split_axis=0, concat_axis=0, tiled=True)
    context = arrived.reshape(req_count * capacity, page_len, 2 * HD)[arrival_index]
    context_keys = context[:, :, :HD].reshape(page_total * page_len, HD)
    context_values = context[:, :, HD:].reshape(page_total * page_len, HD)
    fresh_keys = lax.dynamic_slice_in_dim(new_keys, kv_head * HD, HD, 1)
    fresh_values = lax.dynamic_slice_in_dim(new_values, kv_head * HD, HD, 1)
    all_keys = jnp.concatenate([context_keys, fresh_keys], axis=0)
    all_values = jnp.concatenate([context_values, fresh_values], axis=0)
    masking = attend_masks(
        page_counts[0], last_fill[0], row_counts[0], page_len, page_total, row_total
    )
    query_rows = queries.reshape(row_total, local_heads, HD)
    scores = jnp.einsum("rhd,kd->hrk", query_rows, all_keys, preferred_element_type=jnp.float32) * (
        1.0 / math.sqrt(HD)
    )
    scores = jnp.where(masking[None], scores, -1e30)
    highest = jnp.max(scores, axis=-1, keepdims=True)
    expo = jnp.exp(scores - highest)
    weights = (expo / jnp.sum(expo, axis=-1, keepdims=True)).astype(jnp.bfloat16)
    attention = jnp.einsum("hrk,kd->rhd", weights, all_values, preferred_element_type=jnp.float32)
    attention = attention.astype(jnp.bfloat16).reshape(row_total, local_heads * HD)
    partial_sum = jnp.dot(attention, out_weight, preferred_element_type=jnp.float32)
    columns = hidden.shape[1]
    summed = lax.psum(partial_sum, "tp")
    squares = jnp.sum(summed * summed, axis=1)
    local_part = lax.dynamic_slice_in_dim(summed, tp_index * columns, columns, 1)
    normed = (
        local_part
        * lax.rsqrt(squares / D + 1e-06)[:, None]
        * attn_gain.astype(jnp.float32)[None, :]
    )
    mixed_state = (hidden.astype(jnp.float32) + normed).astype(jnp.bfloat16)
    gate = lax.psum(jnp.dot(mixed_state, ple_gate_weight, preferred_element_type=jnp.float32), "tp")
    activated = (jax.nn.gelu(gate, approximate=True) * ple_input.astype(jnp.float32)).astype(
        jnp.bfloat16
    )
    lifted = jnp.dot(activated, ple_proj_weight, preferred_element_type=jnp.float32)
    lift_squares = lax.psum(jnp.sum(lifted * lifted, axis=1), "tp")
    lift_normed = (
        lifted
        * lax.rsqrt(lift_squares / D + 1e-06)[:, None]
        * ple_gain.astype(jnp.float32)[None, :]
    )
    return (mixed_state.astype(jnp.float32) + lift_normed).astype(jnp.bfloat16)


def solution(mesh):
    return jax.shard_map(
        shards,
        mesh=mesh,
        in_specs=(
            P("req", "tp"),
            P("req", "tp"),
            P("req", None),
            P("req", None),
            P("req", None, None),
            P("req", None, None),
            P("tp", None),
            P("tp"),
            P("req", None),
            P("tp", None),
            P(None, "tp"),
            P("tp"),
            P("req", None),
            P("req", None),
            P("req", None),
            P("req", None),
            P("req", None),
        ),
        out_specs=P("req", "tp"),
        check_vma=False,
    )
```

profile of v0, /device:TPU:0, one launch (start us, length us, event | category | flops | bytes accessed | tf_op | source)
XLA Modules:
  0.0 293.5 jit_solution(17418125813564555138)
XLA Ops:
  6.5 0.0 copy-start
  6.5 1.0 convert_reduce_fusion.1
  7.5 0.7 iota_compare_fusion.5
  8.2 0.7 add_bitcast_fusion.2
  8.9 0.2 select_reduce_fusion.2
  9.1 0.7 copy.35
  9.7 7.3 %all-to-all-start = ((s32[8,1,6]{2,1,0:T(1,128)}), s32[8,1,6]{2,1,0:T(1,128)S(1)}, u32[]{:S(2)}, u32[]{:S(2)}) async-start(s32[8,1,6]{2,1,0:T(1,128)} %copy.35), calls=%async_computation | async-start | bytes 8192 | tf_op jit(solution)/shard_map/all_to_all | solution.py:73
  17.0 2.2 constant_dynamic-slice_fusion.2
  19.3 2.0 pad_maximum_fusion
  21.2 2.2 all-to-all-done
  23.4 0.1 reshape.180
  23.5 4.4 %gather_fusion = bf16[48,64,512]{2,1,0:T(8,128)(2,1)} fusion(bf16[48,64,512]{2,1,0:T(8,128)(2,1)} %pad_maximum_fusion, s32[1024]{0:T(1024)S(1)} %pad_clamp_fusion.1), kind=kCustom, calls=%fused_computation | custom fusion | bytes 6291648 | tf_op jit(solution)/shard_map/gather | solution.py:79
  28.0 0.0 copy-start.8
  28.0 0.0 copy-start.10
  28.0 0.0 copy-start.4
  28.0 0.0 copy-start.9
  28.0 0.0 copy-start.7
  28.0 4.6 %all-to-all-start.1 = ((bf16[8,6,64,512]{3,2,1,0:T(8,128)(2,1)}), bf16[8,6,64,512]{3,2,1,0:T(8,128)(2,1)}, u32[]{:S(2)}, u32[]{:S(2)}) async-start(bf16[8,6,64,512]{3,2,1,0:T(8,128)(2,1)} %bitcast.52), calls=%async_computation.1 | async-start | bytes 6291456 | tf_op jit(solution)/shard_map/all_to_all | solution.py:80
  32.6 0.0 all-reduce.3.cloned.1.call-start
  32.6 0.0 copy-done.8
  32.6 0.2 reduce-window_1_clone.1
  32.8 0.0 copy-done.10
  32.8 0.2 reduce-window_clone.1
  33.0 0.0 copy-done.4
  33.0 1.0 constant_dynamic-slice_fusion
  34.0 0.1 copy.44
  34.1 0.0 copy-done.9
  34.2 0.1 convert_reduce_fusion.2
  34.3 0.0 copy-done.7
  34.3 0.1 convert_reduce_fusion
  34.4 0.1 select_reduce_fusion.1
  34.6 0.2 fusion.12
  34.8 2.4 compare_and_fusion
  37.1 1.7 pad_add_fusion
  38.8 63.4 %all-to-all-done.1 = bf16[8,6,64,512]{3,2,1,0:T(8,128)(2,1)} async-done(((bf16[8,6,64,512]{3,2,1,0:T(8,128)(2,1)}), bf16[8,6,64,512]{3,2,1,0:T(8,128)(2,1)}, u32[]{:S(2)}, u32[]{:S(2)}) %all-to-all-start.1) | async-done | bytes 3145760 | tf_op jit(solution)/shard_map/all_to_all | solution.py:80
  102.2 4.4 %gather_fusion.1 = bf16[48,64,512]{2,1,0:T(8,128)(2,1)} fusion(bf16[48,64,512]{2,1,0:T(8,128)(2,1)} %bitcast.4, s32[1024]{0:T(1024)S(1)} %pad_clamp_fusion), kind=kCustom, calls=%fused_computation.1 | custom fusion | bytes 6291648 | tf_op jit(solution)/shard_map/gather | solution.py:81
  106.7 4.0 %fusion.49 = (bf16[48,64,256]{2,1,0:T(8,128)(2,1)}, bf16[48,64,256]{2,1,0:T(8,128)(2,1)}) fusion(bf16[48,64,512]{2,1,0:T(8,128)(2,1)} %gather_fusion.1), kind=kLoop, calls=%fused_computation.97 | loop fusion | bytes 6291456 | tf_op jit(solution)/shard_map/slice | solution.py:83
  110.6 0.0 copy-start.1
  110.6 2.7 copy.37
  113.3 0.0 copy-done.1
  113.3 8.7 %fusion.8 = f32[3584,512,2]{1,0,2:T(8,128)} fusion(bf16[512,256]{1,0:T(8,128)(2,1)S(1)} %get-tuple-element.15, bf16[3072,256]{1,0:T(8,128)(2,1)} %bitcast.53, bf16[64,2,8,256]{3,2,1,0:T(8,128)(2,1)S(1)} %bitcast.55), kind=kOutput, calls=%fused_computation.19 | convolution fusion | flops 1882718208 | bytes 17039360 | tf_op jit(solution)/shard_map/rhd,kd->hrk/dot_general | solution.py:92
  122.0 17.1 %fusion.50 = (f32[2,512]{1,0:T(2,128)S(1)}, f32[2,512,3584]{1,2,0:T(8,128)}) fusion(f32[3584,512,2]{1,0,2:T(8,128)} %fusion.8, pred[512,3584]{0,1:T(8,128)(4,1)} %pad_add_fusion), kind=kOutput, calls=%fused_computation.98 | output fusion | flops 22023680 | bytes 31199232 | tf_op jit(solution)/shard_map/sub | solution.py:97
  139.1 7.7 %fusion.11 = bf16[256,2,512]{2,0,1:T(8,128)(2,1)S(1)} fusion(f32[2,512,3584]{1,2,0:T(8,128)} %get-tuple-element.12, f32[2,512]{1,0:T(2,128)S(1)} %get-tuple-element.11, bf16[512,256]{0,1:T(8,128)(2,1)S(1)} %copy.44, bf16[3072,256]{0,1:T(8,128)(2,1)} %copy.37), kind=kOutput, calls=%fused_computation.22 | convolution fusion | flops 1890320384 | bytes 17043456 | tf_op jit(solution)/shard_map/hrk,kd->rhd/dot_general | solution.py:99
  146.8 0.0 copy-done
  146.9 3.2 %fusion.51 = f32[512,2048]{1,0:T(8,128)} fusion(bf16[512,512]{0,1:T(8,128)(2,1)S(1)} %bitcast.56, bf16[512,2048]{1,0:T(8,128)(2,1)S(1)} %copy-done), kind=kOutput, calls=%fused_computation.99 | convolution fusion | flops 1073741824 | bytes 6815744 | tf_op jit(solution)/shard_map/dot_general | solution.py:101
  150.1 0.0 all-reduce.3.cloned.1.call-update
  150.1 0.0 copy-start.2
  150.1 0.0 all-reduce.5.cloned.1.call-start
  150.2 0.6 copy-done.5
  150.8 0.0 copy-start.3
  150.8 0.0 copy-start.6
  150.8 84.0 %all-reduce.3.cloned.1.call-done = f32[512,2048]{1,0:T(8,128)} async-done(((f32[512,2048]{1,0:T(8,128)}), f32[512,2048]{1,0:T(8,128)}) %all-reduce.3.cloned.1.call-update) | async-done | bytes 4194320 | tf_op jit(solution)/shard_map/psum | solution.py:103
  234.8 2.5 multiply_reduce_fusion
  237.4 0.0 copy-done.2
  237.4 1.5 add_convert_fusion.1
  238.8 0.0 copy-done.3
  238.8 1.1 fusion.52
  239.9 0.0 all-reduce.5.cloned.1.call-update
  239.9 0.0 copy-done.6
  240.0 33.5 %all-reduce.5.cloned.1.call-done = f32[512,256]{1,0:T(8,128)} async-done(((f32[512,256]{1,0:T(8,128)}), f32[512,256]{1,0:T(8,128)}) %all-reduce.5.cloned.1.call-update) | async-done | bytes 524304 | tf_op jit(solution)/shard_map/psum | solution.py:112
  273.4 2.7 multiply_reduce_fusion.1
  276.1 2.6 copy.40
  278.7 5.7 %psum.23 = f32[512]{0:T(512)S(1)} all-reduce(f32[512]{0:T(512)S(1)} %get-tuple-element.13), channel_id=1, replica_groups=mesh['req'=8,'tp'=4] {'tp'}, use_global_device_ids=true, to_apply=%region_14.15 | all-reduce | flops 512 | bytes 4096 | tf_op jit(solution)/shard_map/psum | solution.py:117
  284.4 2.2 add_convert_fusion
  (17 shorter events, 0.1 us)
Async XLA Ops:
  6.5 140.3 %copy-start = (bf16[512,2048]{1,0:T(8,128)(2,1)S(1)}, bf16[512,2048]{1,0:T(8,128)(2,1)}, u32[]{:S(2)}) copy-start(bf16[512,2048]{1,0:T(8,128)(2,1)} %param.23) | copy-start | bytes 6291460
  9.7 13.7 %all-to-all-start = ((s32[8,1,6]{2,1,0:T(1,128)}), s32[8,1,6]{2,1,0:T(1,128)S(1)}, u32[]{:S(2)}, u32[]{:S(2)}) async-start(s32[8,1,6]{2,1,0:T(1,128)} %copy.35), calls=%async_computation | async-start | bytes 8192 | tf_op jit(solution)/shard_map/all_to_all | solution.py:73
  28.0 4.7 %copy-start.8 = (s32[1,8]{1,0:T(1,128)S(1)}, s32[1,8]{1,0:T(1,128)}, u32[]{:S(2)}) copy-start(s32[1,8]{1,0:T(1,128)} %param.31) | copy-start | bytes 100
  28.0 4.9 %copy-start.10 = (s32[1,8]{1,0:T(1,128)S(1)}, s32[1,8]{1,0:T(1,128)}, u32[]{:S(2)}) copy-start(s32[1,8]{1,0:T(1,128)} %param.33) | copy-start | bytes 100
  28.0 5.0 %copy-start.4 = (bf16[512,512]{1,0:T(8,128)(2,1)S(1)}, bf16[512,512]{1,0:T(8,128)(2,1)}, u32[]{:S(2)}) copy-start(bf16[512,512]{1,0:T(8,128)(2,1)} %param.19) | copy-start | bytes 1572868
  28.0 6.2 %copy-start.9 = (s32[48,1]{0,1:T(1,128)S(1)}, s32[48,1]{0,1:T(1,128)}, u32[]{:S(2)}) copy-start(s32[48,1]{0,1:T(1,128)} %param.29) | copy-start | bytes 580
  28.0 6.3 %copy-start.7 = (s32[1,8]{1,0:T(1,128)S(1)}, s32[1,8]{1,0:T(1,128)}, u32[]{:S(2)}) copy-start(s32[1,8]{1,0:T(1,128)} %param.32) | copy-start | bytes 100
  28.0 74.2 %all-to-all-start.1 = ((bf16[8,6,64,512]{3,2,1,0:T(8,128)(2,1)}), bf16[8,6,64,512]{3,2,1,0:T(8,128)(2,1)}, u32[]{:S(2)}, u32[]{:S(2)}) async-start(bf16[8,6,64,512]{3,2,1,0:T(8,128)(2,1)} %bitcast.52), calls=%async_computation.1 | async-start | bytes 6291456 | tf_op jit(solution)/shard_map/all_to_all | solution.py:80
  32.6 202.2 %all-reduce.3.cloned.1.call-start = ((), (), s32[]{:S(2)}) async-start(), calls=%async_computation.2 | async-start | bytes 8388608 | tf_op jit(solution)/shard_map/psum | solution.py:103
  110.6 2.7 copy-start.1
  150.1 0.7 copy-start.5
  150.1 87.2 %copy-start.2 = (bf16[512,512]{1,0:T(8,128)(2,1)S(1)}, bf16[512,512]{1,0:T(8,128)(2,1)}, u32[]{:S(2)}) copy-start(bf16[512,512]{1,0:T(8,128)(2,1)} %param.17) | copy-start | bytes 1572868
  150.1 123.3 %all-reduce.5.cloned.1.call-start = ((), (), s32[]{:S(2)}) async-start(), calls=%async_computation.3 | async-start | bytes 1048576 | tf_op jit(solution)/shard_map/psum | solution.py:112
  150.8 88.0 %copy-start.3 = (bf16[512,256]{1,0:T(8,128)(2,1)S(1)}, bf16[512,256]{1,0:T(8,128)(2,1)}, u32[]{:S(2)}) copy-start(bf16[512,256]{1,0:T(8,128)(2,1)} %param.26) | copy-start | bytes 786436
  150.8 89.2 %copy-start.6 = (bf16[512]{0:T(512)(128)(2,1)S(1)}, bf16[512]{0:T(512)(128)(2,1)}, u32[]{:S(2)}) copy-start(bf16[512]{0:T(512)(128)(2,1)} %param.28) | copy-start | bytes 3076
Sparse Core Ops, SparseCore 0:
  150.3 84.5 all-reduce.2
  240.1 33.3 all-reduce.4
where the time goes:
time: 294 us
  waiting for transfers between devices  183 us (62%)
  other arithmetic  32.8 us (11%)
  matrix products  23.5 us (8%)
  local copies, waits for them, and re-layouts  22.9 us (8%)
  between operations  13.6 us (5%)
  starting transfers between devices  11.9 us (4%)
  blocking collectives  5.73 us (2%)
    psum x1, waiting for transfers between devices, shards(): summed = lax.psum(partial_sum, 'tp')  84 us
    all_to_all x1, waiting for transfers between devices, shards(): lax.all_to_all(outgoing, 'req', split_axis=0, concat_axis=0, tiled=True)  63.4 us
    psum x1, waiting for transfers between devices, shards(): lax.psum(jnp.dot(mixed_state, ple_gate_weight, preferred_element_type=jnp...  33.5 us
    sub x1, other arithmetic, shards(): expo = jnp.exp(scores - highest)  17.1 us
    dot_general x1, matrix products, shards(): jnp.einsum('rhd,kd->hrk', query_rows, all_keys, preferred_element_type=jn...  8.73 us
    dot_general x1, matrix products, shards(): jnp.einsum('hrk,kd->rhd', weights, all_values, preferred_element_type=jnp...  7.72 us
    all_to_all x1, starting transfers between devices, shards(): lax.all_to_all(request_table, 'req', split_axis=0, concat_axis=0, tiled=T...  7.28 us
  transfers between devices with their start and end apart: 4, of which 4 were waited for; matrix products, arithmetic and copies ran while one was open for 4% of the time, Pallas kernels for 0%

commit v1 on v0

--- a/solution.py
+++ b/solution.py
@@ -100,7 +100,11 @@
     attention = attention.astype(jnp.bfloat16).reshape(row_total, local_heads * HD)
     partial_sum = jnp.dot(attention, out_weight, preferred_element_type=jnp.float32)
     columns = hidden.shape[1]
-    summed = lax.psum(partial_sum, "tp")
+
+    def task_touch(message, bus_axis):
+        return lax.all_gather(message, bus_axis).sum(axis=0)
+
+    summed = task_touch(partial_sum, "tp")
     squares = jnp.sum(summed * summed, axis=1)
     local_part = lax.dynamic_slice_in_dim(summed, tp_index * columns, columns, 1)
     normed = (

time: 294 us -> 325 us (1.11)
  waiting for transfers between devices: 183 us -> 202 us
  other arithmetic: 32.8 us -> 42.3 us
    all_gather x0 -> x1, waiting for transfers between devices: none -> 103 us  [task_touch(): return lax.all_gather(message, bus_axis).sum(axis=0)]
    psum x1 -> x0, waiting for transfers between devices: 84 us -> none  [shards(): summed = lax.psum(partial_sum, 'tp')]
    reduce_sum x0 -> x1, other arithmetic: none -> 10.1 us  [task_touch(): return lax.all_gather(message, bus_axis).sum(axis=0)]
  transfers between devices with their start and end apart: 4 -> 4, of which waited for: 4 -> 4; matrix products, arithmetic and copies ran while one was open for 4% -> 3% of each run, Pallas kernels for 0% -> 0%
where the time goes in v1:
time: 325 us; the launch traced here: 324 us
  waiting for transfers between devices  202 us (62%)
  other arithmetic  42.3 us (13%)
  local copies, waits for them, and re-layouts  25.1 us (8%)
  matrix products  23.4 us (7%)
  between operations  13.6 us (4%)
  starting transfers between devices  12.1 us (4%)
  blocking collectives  5.73 us (2%)
    all_gather x1, waiting for transfers between devices, task_touch(): return lax.all_gather(message, bus_axis).sum(axis=0)  103 us
    all_to_all x1, waiting for transfers between devices, shards(): lax.all_to_all(outgoing, 'req', split_axis=0, concat_axis=0, tiled=True)  63.4 us
    psum x1, waiting for transfers between devices, shards(): lax.psum(jnp.dot(mixed_state, ple_gate_weight, preferred_element_type=jnp...  33.3 us
    sub x1, other arithmetic, shards(): expo = jnp.exp(scores - highest)  17.1 us
    reduce_sum x1, other arithmetic, task_touch(): return lax.all_gather(message, bus_axis).sum(axis=0)  10.1 us
    dot_general x1, matrix products, shards(): jnp.einsum('rhd,kd->hrk', query_rows, all_keys, preferred_element_type=jn...  8.73 us
    dot_general x1, matrix products, shards(): jnp.einsum('hrk,kd->rhd', weights, all_values, preferred_element_type=jnp...  7.72 us
    all_to_all x1, starting transfers between devices, shards(): lax.all_to_all(request_table, 'req', split_axis=0, concat_axis=0, tiled=T...  7.28 us
  transfers between devices with their start and end apart: 4, of which 4 were waited for; matrix products, arithmetic and copies ran while one was open for 3% of the time, Pallas kernels for 0%

profile of v1, /device:TPU:0, one launch (start us, length us, event | category | flops | bytes accessed | tf_op | source)
XLA Modules:
  0.0 324.3 jit_solution(11310288367521696382)
XLA Ops:
  6.5 0.0 copy-start
  6.5 1.0 convert_reduce_fusion.1
  7.5 0.7 iota_compare_fusion.5
  8.2 0.7 add_bitcast_fusion.2
  8.9 0.2 select_reduce_fusion.2
  9.1 0.7 copy.40
  9.7 7.3 %all-to-all-start = ((s32[8,1,6]{2,1,0:T(1,128)}), s32[8,1,6]{2,1,0:T(1,128)S(1)}, u32[]{:S(2)}, u32[]{:S(2)}) async-start(s32[8,1,6]{2,1,0:T(1,128)} %copy.40), calls=%async_computation | async-start | bytes 8192 | tf_op jit(solution)/shard_map/all_to_all | solution.py:73
  17.0 2.2 constant_dynamic-slice_fusion.3
  19.3 2.0 pad_maximum_fusion
  21.2 2.2 all-to-all-done
  23.4 0.1 reshape.180
  23.5 4.4 %gather_fusion = bf16[48,64,512]{2,1,0:T(8,128)(2,1)} fusion(bf16[48,64,512]{2,1,0:T(8,128)(2,1)} %pad_maximum_fusion, s32[1024]{0:T(1024)S(1)} %pad_clamp_fusion.1), kind=kCustom, calls=%fused_computation | custom fusion | bytes 6291648 | tf_op jit(solution)/shard_map/gather | solution.py:79
  28.0 0.0 copy-start.8
  28.0 0.0 copy-start.11
  28.0 0.0 copy-start.7
  28.0 4.6 %all-to-all-start.1 = ((bf16[8,6,64,512]{3,2,1,0:T(8,128)(2,1)}), bf16[8,6,64,512]{3,2,1,0:T(8,128)(2,1)}, u32[]{:S(2)}, u32[]{:S(2)}) async-start(bf16[8,6,64,512]{3,2,1,0:T(8,128)(2,1)} %bitcast.54), calls=%async_computation.1 | async-start | bytes 6291456 | tf_op jit(solution)/shard_map/all_to_all | solution.py:80
  32.6 0.0 all-gather.3.cloned.1.call-start
  32.6 0.0 copy-done.8
  32.6 0.2 reduce-window_1_clone.1
  32.8 0.0 copy-done.11
  32.8 0.2 reduce-window_clone.1
  33.0 0.0 copy-done.4
  33.0 1.0 constant_dynamic-slice_fusion
  34.0 0.1 copy.50
  34.1 0.0 copy-done.10
  34.2 0.1 convert_reduce_fusion.2
  34.3 0.0 copy-done.7
  34.3 0.1 convert_reduce_fusion
  34.4 0.1 select_reduce_fusion.1
  34.6 0.2 fusion.12
  34.8 2.4 compare_and_fusion
  37.1 1.7 pad_add_fusion
  38.8 63.4 %all-to-all-done.1 = bf16[8,6,64,512]{3,2,1,0:T(8,128)(2,1)} async-done(((bf16[8,6,64,512]{3,2,1,0:T(8,128)(2,1)}), bf16[8,6,64,512]{3,2,1,0:T(8,128)(2,1)}, u32[]{:S(2)}, u32[]{:S(2)}) %all-to-all-start.1) | async-done | bytes 3145760 | tf_op jit(solution)/shard_map/all_to_all | solution.py:80
  102.2 4.4 %gather_fusion.1 = bf16[48,64,512]{2,1,0:T(8,128)(2,1)} fusion(bf16[48,64,512]{2,1,0:T(8,128)(2,1)} %bitcast.4, s32[1024]{0:T(1024)S(1)} %pad_clamp_fusion), kind=kCustom, calls=%fused_computation.1 | custom fusion | bytes 6291648 | tf_op jit(solution)/shard_map/gather | solution.py:81
  106.7 4.0 %fusion.49 = (bf16[48,64,256]{2,1,0:T(8,128)(2,1)}, bf16[48,64,256]{2,1,0:T(8,128)(2,1)}) fusion(bf16[48,64,512]{2,1,0:T(8,128)(2,1)} %gather_fusion.1), kind=kLoop, calls=%fused_computation.98 | loop fusion | bytes 6291456 | tf_op jit(solution)/shard_map/slice | solution.py:83
  110.6 2.7 copy.42
  113.3 0.0 copy-done.1
  113.3 8.7 %fusion.8 = f32[3584,512,2]{1,0,2:T(8,128)} fusion(bf16[512,256]{1,0:T(8,128)(2,1)S(1)} %get-tuple-element.15, bf16[3072,256]{1,0:T(8,128)(2,1)} %bitcast.55, bf16[64,2,8,256]{3,2,1,0:T(8,128)(2,1)S(1)} %bitcast.57), kind=kOutput, calls=%fused_computation.19 | convolution fusion | flops 1882718208 | bytes 17039360 | tf_op jit(solution)/shard_map/rhd,kd->hrk/dot_general | solution.py:92
  122.0 17.1 %fusion.50 = (f32[2,512]{1,0:T(2,128)S(1)}, f32[2,512,3584]{1,2,0:T(8,128)}) fusion(f32[3584,512,2]{1,0,2:T(8,128)} %fusion.8, pred[512,3584]{0,1:T(8,128)(4,1)} %pad_add_fusion), kind=kOutput, calls=%fused_computation.99 | output fusion | flops 22023680 | bytes 31199232 | tf_op jit(solution)/shard_map/sub | solution.py:97
  139.1 7.7 %fusion.11 = bf16[256,2,512]{2,0,1:T(8,128)(2,1)S(1)} fusion(f32[2,512,3584]{1,2,0:T(8,128)} %get-tuple-element.12, f32[2,512]{1,0:T(2,128)S(1)} %get-tuple-element.11, bf16[512,256]{0,1:T(8,128)(2,1)S(1)} %copy.50, bf16[3072,256]{0,1:T(8,128)(2,1)} %copy.42), kind=kOutput, calls=%fused_computation.22 | convolution fusion | flops 1890320384 | bytes 17043456 | tf_op jit(solution)/shard_map/hrk,kd->rhd/dot_general | solution.py:99
  146.8 0.0 copy-done
  146.9 3.2 fusion.51
  150.1 0.0 all-gather.3.cloned.1.call-update
  150.1 0.2 all-reduce.2.cloned.1.call-start
  150.3 0.8 copy-done.2
  151.1 1.0 copy.38
  152.1 0.0 copy-done.5
  152.1 103.1 %all-gather.3.cloned.1.call-done = f32[2048,2048]{1,0:T(8,128)} async-done(((f32[512,2048]{1,0:T(8,128)}), f32[2048,2048]{1,0:T(8,128)}) %all-gather.3.cloned.1.call-update) | async-done | bytes 16777232 | tf_op jit(solution)/shard_map/all_gather | solution.py:105
  255.2 10.1 %reduce_sum.100 = f32[512,2048]{1,0:T(8,128)} reduce(f32[4,512,2048]{2,1,0:T(8,128)} %bitcast.53, f32[]{:T(128)} %constant.91.clone.1), dimensions={0}, to_apply=%region_10.11 | reduce | flops 3145728 | bytes 20971524 | tf_op jit(solution)/shard_map/reduce_sum | solution.py:105
  265.3 2.5 multiply_reduce_fusion
  267.9 1.3 constant_dynamic-slice_fusion.2
  269.2 0.0 copy-start.6
  269.2 1.3 copy.51
  270.6 1.6 add_convert_fusion.1
  272.2 0.0 copy-done.3
  272.2 1.1 fusion.52
  273.3 0.0 all-reduce.2.cloned.1.call-update
  273.3 0.0 copy-done.6
  273.4 33.3 %all-reduce.2.cloned.1.call-done = f32[512,256]{1,0:T(8,128)} async-done(((f32[512,256]{1,0:T(8,128)}), f32[512,256]{1,0:T(8,128)}) %all-reduce.2.cloned.1.call-update) | async-done | bytes 524304 | tf_op jit(solution)/shard_map/psum | solution.py:116
  306.7 0.0 copy-done.9
  306.7 2.6 multiply_reduce_fusion.1
  309.3 5.7 %psum.15 = f32[512]{0:T(512)S(1)} all-reduce(f32[512]{0:T(512)S(1)} %get-tuple-element.13), channel_id=1, replica_groups=mesh['req'=8,'tp'=4] {'tp'}, use_global_device_ids=true, to_apply=%region_14.15 | all-reduce | flops 512 | bytes 4096 | tf_op jit(solution)/shard_map/psum | solution.py:121
  315.0 1.4 add_convert_fusion
  316.4 1.0 copy.46
  (23 shorter events, 0.1 us)
Async XLA Ops:
  6.5 140.3 %copy-start = (bf16[512,2048]{1,0:T(8,128)(2,1)S(1)}, bf16[512,2048]{1,0:T(8,128)(2,1)}, u32[]{:S(2)}) copy-start(bf16[512,2048]{1,0:T(8,128)(2,1)} %param.23) | copy-start | bytes 6291460
  9.7 13.7 %all-to-all-start = ((s32[8,1,6]{2,1,0:T(1,128)}), s32[8,1,6]{2,1,0:T(1,128)S(1)}, u32[]{:S(2)}, u32[]{:S(2)}) async-start(s32[8,1,6]{2,1,0:T(1,128)} %copy.40), calls=%async_computation | async-start | bytes 8192 | tf_op jit(solution)/shard_map/all_to_all | solution.py:73
  28.0 4.7 %copy-start.8 = (s32[1,8]{1,0:T(1,128)S(1)}, s32[1,8]{1,0:T(1,128)}, u32[]{:S(2)}) copy-start(s32[1,8]{1,0:T(1,128)} %param.31) | copy-start | bytes 100
  28.0 4.9 %copy-start.11 = (s32[1,8]{1,0:T(1,128)S(1)}, s32[1,8]{1,0:T(1,128)}, u32[]{:S(2)}) copy-start(s32[1,8]{1,0:T(1,128)} %param.33) | copy-start | bytes 100
  28.0 5.0 %copy-start.4 = (bf16[512,512]{1,0:T(8,128)(2,1)S(1)}, bf16[512,512]{1,0:T(8,128)(2,1)}, u32[]{:S(2)}) copy-start(bf16[512,512]{1,0:T(8,128)(2,1)} %param.19) | copy-start | bytes 1572868
  28.0 6.2 %copy-start.10 = (s32[48,1]{0,1:T(1,128)S(1)}, s32[48,1]{0,1:T(1,128)}, u32[]{:S(2)}) copy-start(s32[48,1]{0,1:T(1,128)} %param.29) | copy-start | bytes 580
  28.0 6.3 %copy-start.7 = (s32[1,8]{1,0:T(1,128)S(1)}, s32[1,8]{1,0:T(1,128)}, u32[]{:S(2)}) copy-start(s32[1,8]{1,0:T(1,128)} %param.32) | copy-start | bytes 100
  28.0 74.2 %all-to-all-start.1 = ((bf16[8,6,64,512]{3,2,1,0:T(8,128)(2,1)}), bf16[8,6,64,512]{3,2,1,0:T(8,128)(2,1)}, u32[]{:S(2)}, u32[]{:S(2)}) async-start(bf16[8,6,64,512]{3,2,1,0:T(8,128)(2,1)} %bitcast.54), calls=%async_computation.1 | async-start | bytes 6291456 | tf_op jit(solution)/shard_map/all_to_all | solution.py:80
  32.6 222.6 %all-gather.3.cloned.1.call-start = ((), (), s32[]{:S(2)}) async-start(), calls=%async_computation.3 | async-start | bytes 20971520 | tf_op jit(solution)/shard_map/all_gather | solution.py:105
  110.6 2.7 copy-start.1
  150.1 1.0 copy-start.2
  150.1 2.0 copy-start.5
  150.1 156.6 %all-reduce.2.cloned.1.call-start = ((), (), s32[]{:S(2)}) async-start(), calls=%async_computation.2 | async-start | bytes 1048576 | tf_op jit(solution)/shard_map/psum | solution.py:116
  267.9 4.3 %copy-start.3 = (bf16[512,256]{1,0:T(8,128)(2,1)S(1)}, bf16[512,256]{1,0:T(8,128)(2,1)}, u32[]{:S(2)}) copy-start(bf16[512,256]{1,0:T(8,128)(2,1)} %param.26) | copy-start | bytes 786436
  269.2 4.1 %copy-start.6 = (bf16[512]{0:T(512)(128)(2,1)S(1)}, bf16[512]{0:T(512)(128)(2,1)}, u32[]{:S(2)}) copy-start(bf16[512]{0:T(512)(128)(2,1)} %param.28) | copy-start | bytes 3076
  270.5 36.1 %copy-start.9 = (bf16[256,512]{1,0:T(8,128)(2,1)S(1)}, bf16[256,512]{1,0:T(8,128)(2,1)}, u32[]{:S(2)}) copy-start(bf16[256,512]{1,0:T(8,128)(2,1)} %param.27) | copy-start | bytes 786436
Sparse Core Ops, SparseCore 0:
  150.2 104.9 all-gather.2
  273.5 33.1 all-reduce.1
